TPU v7x, 256 devices: a whole 4x4x8 slice. The times are simulated.
256 devices in a mesh: req: 32 (over z, x), tp: 8 (over y, core).
Axes of the slice: x: 4, y: 4, z: 8, core: 2. Of those that a mesh axis runs over, the one named last changes fastest.
Arguments:
- hidden: bfloat16 [8192, 2048], P('req'), may hold values from -6 to 6
- kv_cache: bfloat16 [2, 1024, 128, 2048], P(None, 'req', None, 'tp'), may hold values from -64 to 64
- page_table: int32 [128, 8], P('req'), may hold values from 0 to 31, as said below
- cache_lens: int32 [128], P('req'), may hold values from 1 to 1024
- parents: int32 [128, 64], P('req'), may hold values from 0 to 62, as said below
- accepted: int32 [128, 8], P('req'), may hold values from 0 to 14, as said below
- attn_gain: float32 [2048], replicated, may hold values from 0.1 to 1.9
- w_qkv: bfloat16 [2048, 3, 2048], P(None, None, 'tp'), may hold values from -0.125 to 0.125
- qk_gain: float32 [2, 2048], P(None, 'tp'), may hold values from 0.5 to 8
- w_out: bfloat16 [2048, 2048], P('tp'), may hold values from -0.5 to 0.5
- moe_gain: float32 [2048], replicated, may hold values from 0.1 to 1.9
- routes: int32 [8192, 8], P('req'), may hold values from 0 to 63, all different within a row; in each aligned block of 256 rows (0 to 255, 256 to 511, ...) at most 40 rows name the same one
- route_weights: float32 [8192, 8], P('req'), may hold values from 0.1 to 1
- w_gate_up: bfloat16 [32, 2048, 2, 2048], P('req', None, None, 'tp'), may hold values from -0.125 to 0.125
- w_down: bfloat16 [32, 2048, 2048], P('req', 'tp'), may hold values from -0.1875 to 0.1875
Outputs:
- output: bfloat16 [8192, 2048], P('req', 'tp')
- accepted_kv: bfloat16 [2, 1024, 2048], P(None, 'req', 'tp')
Inputs may be any that keep to these rules, and one draw needn't show every extreme that they name: `page_table`: values lie in the block of 32 pages of the request's group of 4 requests; within a group every page is used once. parents[r, 0] = 0 and parents[r, j] < j for j >= 1. accepted[r] are the first 8 slots, from the root down, of a path in request r's tree. `routes`: in each aligned block of 256 rows (the tokens of one index of req), no expert is named by more than 40 rows.
All inputs are finite; a program needn't handle non-finite values.
Results may differ from a plain program's by a relative error of at most 0.012.
The roundings to bfloat16 on the way count: a program that leaves them out, or rounds other values in their place, can miss the bound.
Values may be sent and summed in bfloat16 or wider, within the bound.
No kernel may reach another device: no remote copies, remote signals or barrier semaphores. Data moves between devices by JAX's collectives and lax.ppermute only.
A program may use at most 128 MiB of HBM per device.

v0:
```python
import jax
import jax.numpy as jnp
from jax import lax
from jax.sharding import PartitionSpec as P

HD = 128
FFE = 1024
EXPERTS = 64
CAP = 40


norm_eps = 1e-05
rope_base = 10000.0
masked_score = -1e30


def rms_scale(values, gain):
    return values * lax.rsqrt(jnp.mean(values * values, axis=-1, keepdims=True) + norm_eps) * gain


def tree_masks(parents):
    slot_count = parents.shape[-1]
    slot_ids = jnp.arange(slot_count, dtype=jnp.int32)
    parent_hot = (parents[..., :, None] == slot_ids).astype(jnp.float32)
    ancestry = jnp.minimum(jnp.eye(slot_count, dtype=jnp.float32) + parent_hot, 1.0)
    for squaring in range(slot_count.bit_length()):
        ancestry = jnp.minimum(
            jnp.einsum("rij,rjk->rik", ancestry, ancestry, precision=lax.Precision.HIGHEST), 1.0
        )
    depths = jnp.sum(ancestry, axis=-1).astype(jnp.int32) - 1
    return (ancestry, depths)


def rotate(values, positions):
    head_dim = values.shape[-1]
    half_dim = head_dim // 2
    frequency = rope_base ** (-jnp.arange(half_dim, dtype=jnp.float32) * 2.0 / head_dim)
    angles = positions.astype(jnp.float32)[:, None] * frequency[None, :]
    cosine = jnp.cos(angles)[:, None, :]
    sine_part = jnp.sin(angles)[:, None, :]
    first_half = values[..., :half_dim]
    second = values[..., half_dim:]
    return jnp.concatenate(
        [first_half * cosine - second * sine_part, second * cosine + first_half * sine_part],
        axis=-1,
    )


def local(
    hidden,
    kv_cache,
    page_table,
    cache_lens,
    parents,
    accepted,
    attn_gain,
    w_qkv,
    qk_gain,
    w_out,
    moe_gain,
    routes,
    route_weights,
    w_gate_up,
    w_down,
):
    tok_rows, model_width = hidden.shape
    tp_count = lax.axis_size("tp")
    req_count = lax.axis_size("req")
    slice_width = model_width // tp_count
    slice_start = lax.axis_index("tp") * slice_width
    req_local, draft_len = parents.shape
    feat_dev = w_qkv.shape[2]
    local_heads = feat_dev // HD
    ancestry, depths = tree_masks(parents)
    positions = (cache_lens[:, None] + depths).reshape(-1)
    normed_in = rms_scale(hidden.astype(jnp.float32), attn_gain).astype(jnp.bfloat16)
    projected = jnp.dot(
        normed_in, w_qkv.reshape(model_width, 3 * feat_dev), preferred_element_type=jnp.float32
    ).reshape(tok_rows, 3, feat_dev)
    query_raw = projected[:, 0]
    key_raw = projected[:, 1]
    values_new = projected[:, 2].astype(jnp.bfloat16)
    query_total, key_total = lax.psum(
        (jnp.sum(query_raw * query_raw, axis=-1), jnp.sum(key_raw * key_raw, axis=-1)), "tp"
    )
    query_normed = query_raw * lax.rsqrt(query_total[:, None] / model_width + norm_eps) * qk_gain[0]
    key_normed = key_raw * lax.rsqrt(key_total[:, None] / model_width + norm_eps) * qk_gain[1]
    query_rot = rotate(query_normed.reshape(tok_rows, local_heads, HD), positions).astype(
        jnp.bfloat16
    )
    keys_new = rotate(key_normed.reshape(tok_rows, local_heads, HD), positions).astype(jnp.bfloat16)
    page_rows = kv_cache[:, page_table.reshape(-1)]
    context = page_table.shape[1] * kv_cache.shape[2]
    cache_keys = page_rows[0].reshape(req_local, context, local_heads, HD)
    cache_values = page_rows[1].reshape(req_local, context, local_heads, HD)
    query_blocks = query_rot.reshape(req_local, draft_len, local_heads, HD)
    key_blocks = keys_new.reshape(req_local, draft_len, local_heads, HD)
    value_blocks = values_new.reshape(req_local, draft_len, local_heads, HD)
    score_scale = HD ** (-0.5)
    cache_scores = (
        jnp.einsum("rjhd,rchd->rhjc", query_blocks, cache_keys, preferred_element_type=jnp.float32)
        * score_scale
    )
    live_keys = jnp.arange(context, dtype=jnp.int32)[None, :] < cache_lens[:, None]
    cache_scores = jnp.where(live_keys[:, None, None, :], cache_scores, masked_score)
    draft_scores = (
        jnp.einsum("rjhd,rihd->rhji", query_blocks, key_blocks, preferred_element_type=jnp.float32)
        * score_scale
    )
    draft_scores = jnp.where(ancestry[:, None, :, :] > 0.5, draft_scores, masked_score)
    scores = jnp.concatenate([cache_scores, draft_scores], axis=-1)
    row_max = jnp.max(scores, axis=-1, keepdims=True)
    weights = jnp.exp(scores - row_max)
    probabilities = (weights / jnp.sum(weights, axis=-1, keepdims=True)).astype(jnp.bfloat16)
    all_values = jnp.concatenate([cache_values, value_blocks], axis=1)
    attn_heads = (
        jnp.einsum("rhjc,rchd->rjhd", probabilities, all_values, preferred_element_type=jnp.float32)
        .astype(jnp.bfloat16)
        .reshape(tok_rows, feat_dev)
    )
    attn_term = jnp.dot(attn_heads, w_out, preferred_element_type=jnp.float32)
    residual = hidden.astype(jnp.float32) + lax.psum(attn_term, "tp")
    normed_moe = rms_scale(residual, moe_gain).astype(jnp.bfloat16)
    residual_share = lax.dynamic_slice_in_dim(residual, slice_start, slice_width, 1)
    top_k = routes.shape[1]
    experts_here = EXPERTS // req_count
    units_dev = w_gate_up.shape[3]
    local_count = max(1, units_dev // FFE)
    block_units = units_dev // local_count
    first_local = lax.axis_index("tp") * units_dev // FFE
    capacity = CAP
    gate_up_local = w_gate_up[0].reshape(model_width, 2, local_count, block_units)
    down_local = w_down[0].reshape(local_count, block_units, model_width)
    flat_routes = routes.reshape(-1)
    one_hot = (flat_routes[:, None] == jnp.arange(EXPERTS, dtype=jnp.int32)[None, :]).astype(
        jnp.int32
    )
    slot_of = jnp.sum((jnp.cumsum(one_hot, axis=0) - one_hot) * one_hot, axis=1)
    token_ids = jnp.arange(flat_routes.shape[0], dtype=jnp.int32) // top_k
    send_rows = (
        jnp.zeros((EXPERTS, capacity, model_width), jnp.bfloat16)
        .at[flat_routes, slot_of]
        .set(normed_moe[token_ids])
    )
    send_rows = send_rows.reshape(req_count, experts_here, capacity, model_width)
    received = lax.all_to_all(send_rows, "req", split_axis=0, concat_axis=0, tiled=True)
    mine = lax.dynamic_slice_in_dim(received, first_local, local_count, 1)
    gate_up = jnp.einsum(
        "secw,wgeh->secgh", mine, gate_up_local, preferred_element_type=jnp.float32
    )
    activated = (jax.nn.silu(gate_up[..., 0, :]) * gate_up[..., 1, :]).astype(jnp.bfloat16)
    partial_mine = jnp.einsum(
        "sech,ehd->secd", activated, down_local, preferred_element_type=jnp.float32
    )
    partial_out = jnp.zeros(
        (received.shape[0], experts_here, received.shape[2], model_width), jnp.float32
    )
    partial_out = lax.dynamic_update_slice_in_dim(partial_out, partial_mine, first_local, 1)
    shares = lax.psum_scatter(
        partial_out.astype(jnp.bfloat16), "tp", scatter_dimension=3, tiled=True
    )
    returned = lax.all_to_all(shares, "req", split_axis=0, concat_axis=0, tiled=True)
    expert_table = returned.reshape(EXPERTS, capacity, slice_width)
    picked = expert_table[flat_routes, slot_of].reshape(tok_rows, top_k, slice_width)
    mixture = jnp.einsum("tk,tkd->td", route_weights, picked.astype(jnp.float32))
    output = (residual_share + mixture).astype(jnp.bfloat16)
    picked_rows = (jnp.arange(req_local, dtype=jnp.int32)[:, None] * draft_len + accepted).reshape(
        -1
    )
    accepted_kv = jnp.stack(
        [keys_new.reshape(tok_rows, feat_dev)[picked_rows], values_new[picked_rows]]
    )
    return (output, accepted_kv)


def solution(mesh):
    return jax.shard_map(
        local,
        mesh=mesh,
        in_specs=(
            P("req", None),
            P(None, "req", None, "tp"),
            P("req", None),
            P("req"),
            P("req", None),
            P("req", None),
            P(),
            P(None, None, "tp"),
            P(None, "tp"),
            P("tp", None),
            P(),
            P("req", None),
            P("req", None),
            P("req", None, None, "tp"),
            P("req", "tp", None),
        ),
        out_specs=(P("req", "tp"), P(None, "req", "tp")),
        check_vma=False,
    )
```

profile of v0, /device:TPU:32, one launch (start us, length us, event | category | flops | bytes accessed | tf_op | source)
XLA Modules:
  0.0 587.2 jit_solution(11164648943326778122)
XLA Ops:
  7.3 1.6 fusion.13
  8.9 4.8 copy.24
  13.7 3.0 fusion.6
  16.8 0.9 copy-done.5
  21.2 14.9 %all-reduce = (f32[256]{0:T(256)S(1)}, f32[256]{0:T(256)S(1)}) all-reduce(f32[256]{0:T(256)S(1)} %get-tuple-element.3, f32[256]{0:T(256)S(1)} %get-tuple-element.2), channel_id=1, replica_groups=mesh['req'=32,'tp'=8] {'tp'}, use_global_device_ids=true, to_apply=%region_5.0 | all-reduce | flops 512 | bytes 4096 | tf_op jit(solution)/shard_map/psum | solution.py:83
  38.0 0.8 copy.34
  38.9 0.8 copy.27
  39.7 4.9 gather_fusion
  44.7 4.7 fusion.74
  49.4 2.5 reshape_squeeze.8
  51.9 4.0 reshape_squeeze.7
  55.9 1.9 copy.26
  57.8 1.0 fusion.77
  59.7 0.8 fusion.35
  60.9 1.7 fusion.52
  63.3 18.1 %reduce-window.6 = s32[64,16,128]{2,1,0:T(8,128)S(1)} reduce-window(s32[64,16,128]{2,1,0:T(8,128)S(1)} %fusion.50, s32[]{:T(128)} %constant.30.clone.1), window={size=1x1x128 pad=0_0x0_0x127_0}, to_apply=%region_10.11 | reduce-window | flops 16646144 | bytes 1048580 | tf_op jit(solution)/shard_map/reduce-window
  83.0 50.8 %all-reduce.3.cloned.1.call-done = f32[256,2048]{1,0:T(8,128)} async-done(((f32[256,2048]{1,0:T(8,128)}), f32[256,2048]{1,0:T(8,128)}) %all-reduce.3.cloned.1.call-update) | async-done | bytes 2097168 | tf_op jit(solution)/shard_map/psum | solution.py:122
  133.8 1.9 multiply_reduce_fusion
  135.8 1.3 copy-done.1
  137.3 45.0 %scatter_custom_fusion = bf16[2560,2048]{1,0:T(8,128)(2,1)} fusion(s32[2048]{0:T(1024)S(1)} %get-tuple-element.36, bf16[256,2048]{1,0:T(8,128)(2,1)S(1)} %multiply_convert_fusion, s32[2048]{0:T(1024)S(1)} %get-tuple-element.35, bf16[]{:T(256)} %constant.83.clone.1), kind=kCustom, calls=%fused_computation.7 | custom fusion | bytes 10485762
  182.4 10.2 %all-to-all-start = ((bf16[32,2,40,2048]{3,2,1,0:T(8,128)(2,1)}), bf16[32,2,40,2048]{3,2,1,0:T(8,128)(2,1)}, u32[]{:S(2)}, u32[]{:S(2)}) async-start(bf16[32,2,40,2048]{3,2,1,0:T(8,128)(2,1)} %bitcast.134), calls=%async_computation | async-start | bytes 20971520 | tf_op jit(solution)/shard_map/all_to_all | solution.py:146
  192.7 227.6 %all-to-all-done = bf16[32,2,40,2048]{3,2,1,0:T(8,128)(2,1)} async-done(((bf16[32,2,40,2048]{3,2,1,0:T(8,128)(2,1)}), bf16[32,2,40,2048]{3,2,1,0:T(8,128)(2,1)}, u32[]{:S(2)}, u32[]{:S(2)}) %all-to-all-start) | async-done | bytes 10485792 | tf_op jit(solution)/shard_map/all_to_all | solution.py:146
  420.3 4.9 fusion.20
  425.2 5.3 broadcast_in_dim.24
  430.5 3.9 bitcast_dynamic-update-slice_fusion
  434.5 90.4 %reduce-scatter.2.cloned.1.call-done = bf16[32,2,40,256]{3,2,1,0:T(8,128)(2,1)} async-done(((bf16[32,2,40,2048]{3,2,1,0:T(8,128)(2,1)}), bf16[32,2,40,256]{3,2,1,0:T(8,128)(2,1)}) %reduce-scatter.2.cloned.1.call-update) | async-done | bytes 1310736 | tf_op jit(solution)/shard_map/reduce_scatter | solution.py:159
  524.9 10.0 %all-to-all-start.1 = ((bf16[32,2,40,256]{3,2,1,0:T(8,128)(2,1)}), bf16[32,2,40,256]{3,2,1,0:T(8,128)(2,1)S(1)}, u32[]{:S(2)}, u32[]{:S(2)}) async-start(bf16[32,2,40,256]{3,2,1,0:T(8,128)(2,1)} %reduce-scatter.2.cloned.1.call-done), calls=%async_computation.2 | async-start | bytes 2621440 | tf_op jit(solution)/shard_map/all_to_all | solution.py:162
  535.0 0.8 copy.47
  535.8 1.0 slice_bitcast_fusion
  538.9 28.3 %all-to-all-done.1 = bf16[32,2,40,256]{3,2,1,0:T(8,128)(2,1)S(1)} async-done(((bf16[32,2,40,256]{3,2,1,0:T(8,128)(2,1)}), bf16[32,2,40,256]{3,2,1,0:T(8,128)(2,1)S(1)}, u32[]{:S(2)}, u32[]{:S(2)}) %all-to-all-start.1) | async-done | bytes 1310752 | tf_op jit(solution)/shard_map/all_to_all | solution.py:162
  567.2 11.1 %gather_fusion.1 = bf16[2048,256]{1,0:T(8,128)(2,1)S(1)} fusion(bf16[64,40,256]{2,1,0:T(8,128)(2,1)S(1)} %bitcast.133, s32[2048]{0:T(1024)S(1)} %bitcast.132), kind=kCustom, calls=%fused_computation.2 | custom fusion | bytes 2113536 | tf_op jit(solution)/shard_map/gather | solution.py:164
  578.7 1.6 fusion.51
  (114 shorter events, 11.8 us)
Async XLA Ops:
  7.2 423.4 %copy-start = (bf16[1,256,2048]{2,1,0:T(8,128)(2,1)S(1)}, bf16[1,256,2048]{2,1,0:T(8,128)(2,1)}, u32[]{:S(2)}) copy-start(bf16[1,256,2048]{2,1,0:T(8,128)(2,1)} %param.29) | copy-start | bytes 3145732
  7.2 126.6 %all-reduce.3.cloned.1.call-start = ((), (), s32[]{:S(2)}) async-start(), calls=%async_computation.3 | async-start | bytes 4194304 | tf_op jit(solution)/shard_map/psum | solution.py:122
  8.9 4.8 copy-start.2
  8.9 4.8 copy-start.22
  13.7 4.0 copy-start.15
  13.7 4.1 copy-start.16
  13.7 4.3 copy-start.17
  13.7 4.3 copy-start.14
  13.7 4.4 copy-start.18
  16.7 0.9 copy-start.5
  57.8 1.0 copy-start.6
  57.8 1.0 copy-start.7
  57.8 1.0 copy-start.9
  58.8 0.9 copy-start.8
  59.7 1.2 copy-start.4
  60.9 1.8 copy-start.12
  63.2 19.5 %copy-start.20 = (s32[2]{0:T(128)S(1)}, s32[2]{0:T(128)}, u32[]{:S(2)}) copy-start(s32[2]{0:T(128)} %constant.98) | copy-start | bytes 28
  63.2 19.6 %copy-start.19 = (s32[2]{0:T(128)S(1)}, s32[2]{0:T(128)}, u32[]{:S(2)}) copy-start(s32[2]{0:T(128)} %constant.101) | copy-start | bytes 28
  63.3 70.5 %copy-start.3 = (bf16[256,2048]{1,0:T(8,128)(2,1)S(1)}, bf16[256,2048]{1,0:T(8,128)(2,1)}, u32[]{:S(2)}) copy-start(bf16[256,2048]{1,0:T(8,128)(2,1)} %param.15) | copy-start | bytes 3145732
  83.0 54.1 %copy-start.11 = (f32[2048]{0:T(1024)S(1)}, f32[2048]{0:T(1024)}, u32[]{:S(2)}) copy-start(f32[2048]{0:T(1024)} %param.25) | copy-start | bytes 24580
  135.7 1.3 copy-start.1
  182.4 237.9 %copy-start.21 = (bf16[1,2048,2,256]{3,2,1,0:T(2,128)(2,1)S(1)}, bf16[1,2048,2,256]{3,2,1,0:T(2,128)(2,1)}, u32[]{:S(2)}) copy-start(bf16[1,2048,2,256]{3,2,1,0:T(2,128)(2,1)} %param.28) | copy-start | bytes 6291460
  182.4 237.9 %all-to-all-start = ((bf16[32,2,40,2048]{3,2,1,0:T(8,128)(2,1)}), bf16[32,2,40,2048]{3,2,1,0:T(8,128)(2,1)}, u32[]{:S(2)}, u32[]{:S(2)}) async-start(bf16[32,2,40,2048]{3,2,1,0:T(8,128)(2,1)} %bitcast.134), calls=%async_computation | async-start | bytes 20971520 | tf_op jit(solution)/shard_map/all_to_all | solution.py:146
  192.6 332.3 %reduce-scatter.2.cloned.1.call-start = ((), (), s32[]{:S(2)}) async-start(), calls=%async_computation.4 | async-start | bytes 11796480 | tf_op jit(solution)/shard_map/reduce_scatter | solution.py:159
  434.5 100.4 %copy-start.13 = (f32[256,8]{0,1:T(8,128)S(1)}, f32[256,8]{0,1:T(8,128)}, u32[]{:S(2)}) copy-start(f32[256,8]{0,1:T(8,128)} %param.27) | copy-start | bytes 24580
  524.9 42.3 %all-to-all-start.1 = ((bf16[32,2,40,256]{3,2,1,0:T(8,128)(2,1)}), bf16[32,2,40,256]{3,2,1,0:T(8,128)(2,1)S(1)}, u32[]{:S(2)}, u32[]{:S(2)}) async-start(bf16[32,2,40,256]{3,2,1,0:T(8,128)(2,1)} %reduce-scatter.2.cloned.1.call-done), calls=%async_computation.2 | async-start | bytes 2621440 | tf_op jit(solution)/shard_map/all_to_all | solution.py:162
  567.2 11.1 %copy-start.10 = (bf16[256,8,1]{1,2,0:T(2,128)(2,1)S(1)}, bf16[256,8,1]{1,2,0:T(2,128)(2,1)}, u32[]{:S(2)}) copy-start(bf16[256,8,1]{1,2,0:T(2,128)(2,1)} %copy.47) | copy-start | bytes 12292
Sparse Core Ops, SparseCore 0:
  62.8 70.9 all-reduce.2
  434.6 90.2 reduce-scatter.1
where the time goes:
time: 589 us; the launch traced here: 587 us
  waiting for transfers between devices  397 us (67%)
  local copies, waits for them, and re-layouts  95.6 us (16%)
  other arithmetic  26.6 us (5%)
  starting transfers between devices  20.3 us (3%)
  matrix products  18.1 us (3%)
  blocking collectives  14.9 us (3%)
  between operations  14.7 us (2%)
    all_to_all x1, waiting for transfers between devices, local(): lax.all_to_all(send_rows, 'req', split_axis=0, concat_axis=0, tiled=True)  228 us
    reduce_scatter x1, waiting for transfers between devices, local(): lax.psum_scatter(partial_out.astype(jnp.bfloat16), 'tp', scatter_dimensio...  90.4 us
    unnamed x50, local copies, waits for them, and re-layouts  53.3 us
    psum x1, waiting for transfers between devices, local(): residual = hidden.astype(jnp.float32) + lax.psum(attn_term, 'tp')  50.8 us
    all_to_all x1, waiting for transfers between devices, local(): lax.all_to_all(shares, 'req', split_axis=0, concat_axis=0, tiled=True)  28.3 us
    another operation x4, other arithmetic  18.6 us
    psum x1, blocking collectives, local(): lax.psum((jnp.sum(query_raw * query_raw, axis=-1), jnp.sum(key_raw * key_...  14.9 us
  transfers between devices with their start and end apart: 4, of which 4 were waited for; matrix products, arithmetic and copies ran while one was open for 4% of the time, Pallas kernels for 0%

commit v1 on v0

--- a/solution.py
+++ b/solution.py
@@ -1,12 +1,13 @@
 import jax
 import jax.numpy as jnp
 from jax import lax
-from jax.sharding import PartitionSpec as P
+from jax.sharding import Mesh, PartitionSpec as P
 
 HD = 128
 FFE = 1024
 EXPERTS = 64
 CAP = 40
+TP = ("th", "tl", "tc")
 
 
 norm_eps = 1e-05
@@ -64,10 +65,13 @@
     w_down,
 ):
     tok_rows, model_width = hidden.shape
-    tp_count = lax.axis_size("tp")
+    th = lax.axis_index("th")
+    tl = lax.axis_index("tl")
+    tc = lax.axis_index("tc")
+    tp_count = lax.axis_size(TP)
     req_count = lax.axis_size("req")
     slice_width = model_width // tp_count
-    slice_start = lax.axis_index("tp") * slice_width
+    slice_start = ((th * lax.axis_size("tl") + tl) * lax.axis_size("tc") + tc) * slice_width
     req_local, draft_len = parents.shape
     feat_dev = w_qkv.shape[2]
     local_heads = feat_dev // HD
@@ -81,7 +85,7 @@
     key_raw = projected[:, 1]
     values_new = projected[:, 2].astype(jnp.bfloat16)
     query_total, key_total = lax.psum(
-        (jnp.sum(query_raw * query_raw, axis=-1), jnp.sum(key_raw * key_raw, axis=-1)), "tp"
+        (jnp.sum(query_raw * query_raw, axis=-1), jnp.sum(key_raw * key_raw, axis=-1)), TP
     )
     query_normed = query_raw * lax.rsqrt(query_total[:, None] / model_width + norm_eps) * qk_gain[0]
     key_normed = key_raw * lax.rsqrt(key_total[:, None] / model_width + norm_eps) * qk_gain[1]
@@ -119,50 +123,55 @@
         .reshape(tok_rows, feat_dev)
     )
     attn_term = jnp.dot(attn_heads, w_out, preferred_element_type=jnp.float32)
-    residual = hidden.astype(jnp.float32) + lax.psum(attn_term, "tp")
+    residual = hidden.astype(jnp.float32) + lax.psum(attn_term, TP)
     normed_moe = rms_scale(residual, moe_gain).astype(jnp.bfloat16)
     residual_share = lax.dynamic_slice_in_dim(residual, slice_start, slice_width, 1)
-    top_k = routes.shape[1]
     experts_here = EXPERTS // req_count
-    units_dev = w_gate_up.shape[3]
-    local_count = max(1, units_dev // FFE)
-    block_units = units_dev // local_count
-    first_local = lax.axis_index("tp") * units_dev // FFE
+    tok_ids = jnp.arange(tok_rows, dtype=jnp.int32)
+    route_hot = (routes[:, :, None] == jnp.arange(EXPERTS, dtype=jnp.int32)).astype(jnp.float32)
+    per_token = jnp.sum(route_hot, axis=1)
+    weight_of = jnp.sum(route_weights[:, :, None] * route_hot, axis=1)
+    earlier = (tok_ids[:, None] > tok_ids[None, :]).astype(jnp.bfloat16)
+    slot_of = jnp.dot(earlier, per_token.astype(jnp.bfloat16), preferred_element_type=jnp.float32)
     capacity = CAP
-    gate_up_local = w_gate_up[0].reshape(model_width, 2, local_count, block_units)
-    down_local = w_down[0].reshape(local_count, block_units, model_width)
-    flat_routes = routes.reshape(-1)
-    one_hot = (flat_routes[:, None] == jnp.arange(EXPERTS, dtype=jnp.int32)[None, :]).astype(
-        jnp.int32
-    )
-    slot_of = jnp.sum((jnp.cumsum(one_hot, axis=0) - one_hot) * one_hot, axis=1)
-    token_ids = jnp.arange(flat_routes.shape[0], dtype=jnp.int32) // top_k
-    send_rows = (
-        jnp.zeros((EXPERTS, capacity, model_width), jnp.bfloat16)
-        .at[flat_routes, slot_of]
-        .set(normed_moe[token_ids])
-    )
-    send_rows = send_rows.reshape(req_count, experts_here, capacity, model_width)
-    received = lax.all_to_all(send_rows, "req", split_axis=0, concat_axis=0, tiled=True)
-    mine = lax.dynamic_slice_in_dim(received, first_local, local_count, 1)
+    cap_ids = jnp.arange(capacity, dtype=jnp.float32)
+    picked_here = lax.dynamic_index_in_dim(
+        per_token.reshape(tok_rows, req_count, experts_here), th, axis=2, keepdims=False
+    ).T
+    slot_here = lax.dynamic_index_in_dim(
+        slot_of.reshape(tok_rows, req_count, experts_here), th, axis=2, keepdims=False
+    ).T
+    select = jnp.where(
+        (picked_here[:, None, :] > 0.5) & (slot_here[:, None, :] == cap_ids[None, :, None]), 1.0, 0.0
+    ).astype(jnp.bfloat16)
+    half_width = model_width // 2
+    normed_half = lax.dynamic_slice_in_dim(normed_moe, tc * half_width, half_width, 1)
+    send_rows = jnp.einsum(
+        "ict,tw->icw", select, normed_half, preferred_element_type=jnp.float32
+    ).astype(jnp.bfloat16)
+    received = lax.all_to_all(send_rows, "req", 0, 0, tiled=True)
+    rows = lax.all_gather(received, "tc", axis=2, tiled=True)
     gate_up = jnp.einsum(
-        "secw,wgeh->secgh", mine, gate_up_local, preferred_element_type=jnp.float32
+        "scw,wgu->scgu", rows, w_gate_up[0], preferred_element_type=jnp.float32
     )
     activated = (jax.nn.silu(gate_up[..., 0, :]) * gate_up[..., 1, :]).astype(jnp.bfloat16)
-    partial_mine = jnp.einsum(
-        "sech,ehd->secd", activated, down_local, preferred_element_type=jnp.float32
-    )
-    partial_out = jnp.zeros(
-        (received.shape[0], experts_here, received.shape[2], model_width), jnp.float32
-    )
-    partial_out = lax.dynamic_update_slice_in_dim(partial_out, partial_mine, first_local, 1)
-    shares = lax.psum_scatter(
-        partial_out.astype(jnp.bfloat16), "tp", scatter_dimension=3, tiled=True
-    )
-    returned = lax.all_to_all(shares, "req", split_axis=0, concat_axis=0, tiled=True)
-    expert_table = returned.reshape(EXPERTS, capacity, slice_width)
-    picked = expert_table[flat_routes, slot_of].reshape(tok_rows, top_k, slice_width)
-    mixture = jnp.einsum("tk,tkd->td", route_weights, picked.astype(jnp.float32))
+    units_dev = w_down.shape[1]
+    down = w_down[0].reshape(units_dev, 2, 2, 2, slice_width)
+    partial = jnp.einsum(
+        "scu,uhlkd->shckld", activated, down, preferred_element_type=jnp.float32
+    ).astype(jnp.bfloat16)
+    partial = partial.reshape(req_count, 2, capacity, 4 * slice_width)
+    partial = lax.psum_scatter(partial, "tc", scatter_dimension=3, tiled=True)
+    partial = lax.psum_scatter(partial, "tl", scatter_dimension=3, tiled=True)
+    back = partial.reshape(req_count * 2, capacity, slice_width)
+    returned = lax.all_to_all(back, ("req", "th"), 0, 0, tiled=True)
+    combine = weight_of[:, :, None] * (slot_of[:, :, None] == cap_ids[None, None, :])
+    mixture = jnp.dot(
+        combine.reshape(tok_rows, EXPERTS * capacity),
+        returned.reshape(EXPERTS * capacity, slice_width).astype(jnp.float32),
+        precision=lax.Precision.HIGHEST,
+        preferred_element_type=jnp.float32,
+    )
     output = (residual_share + mixture).astype(jnp.bfloat16)
     picked_rows = (jnp.arange(req_local, dtype=jnp.int32)[:, None] * draft_len + accepted).reshape(
         -1
@@ -174,26 +183,29 @@
 
 
 def solution(mesh):
+    req_count = mesh.shape["req"]
+    devices = mesh.devices.reshape(req_count, 2, 2, mesh.shape["tp"] // 4)
+    split_mesh = Mesh(devices, ("req",) + TP)
     return jax.shard_map(
         local,
-        mesh=mesh,
+        mesh=split_mesh,
         in_specs=(
             P("req", None),
-            P(None, "req", None, "tp"),
+            P(None, "req", None, TP),
             P("req", None),
             P("req"),
             P("req", None),
             P("req", None),
             P(),
-            P(None, None, "tp"),
-            P(None, "tp"),
-            P("tp", None),
+            P(None, None, TP),
+            P(None, TP),
+            P(TP, None),
             P(),
             P("req", None),
             P("req", None),
-            P("req", None, None, "tp"),
-            P("req", "tp", None),
+            P("req", None, None, TP),
+            P("req", TP, None),
         ),
-        out_specs=(P("req", "tp"), P(None, "req", "tp")),
+        out_specs=(P("req", TP), P(None, "req", TP)),
         check_vma=False,
     )

time: 589 us -> 380 us (0.65)
  waiting for transfers between devices: 397 us -> 182 us
  blocking collectives: 14.9 us -> 85.2 us
  local copies, waits for them, and re-layouts: 95.6 us -> 52.8 us
  other arithmetic: 26.6 us -> 7 us
  starting transfers between devices: 20.3 us -> 13.1 us
  matrix products: 18.1 us -> 24.1 us
    all_to_all x2 -> x1, waiting for transfers between devices: 256 us -> 32.4 us  [local(): returned = lax.all_to_all(back, ('req', 'th'), 0, 0, tiled=True)]
    all_to_all x0 -> x1, blocking collectives: none -> 70.3 us  [local(): received = lax.all_to_all(send_rows, 'req', 0, 0, tiled=True)]
    unnamed x50 -> x43, local copies, waits for them, and re-layouts: 53.3 us -> 7.29 us
    reduce_scatter x1 -> x2, waiting for transfers between devices: 90.4 us -> 66.1 us  [the longest x1 46.4 us: local(): partial = lax.psum_scatter(partial, 'tl', scatter_dimension=3, tiled=True)]
    another operation x4 -> x1, other arithmetic: 18.6 us -> 0.07 us
    psum x1, waiting for transfers between devices: 50.8 us -> 69.2 us  [local(): residual = hidden.astype(jnp.float32) + lax.psum(attn_term, TP)]
    all_gather x0 -> x1, waiting for transfers between devices: none -> 14.3 us  [local(): rows = lax.all_gather(received, 'tc', axis=2, tiled=True)]
    gather x1 -> x0, local copies, waits for them, and re-layouts: 11.1 us -> none  [local(): expert_table[flat_routes, slot_of].reshape(tok_rows, top_k, slice_width)]
  transfers between devices with their start and end apart: 4 -> 5, of which waited for: 4 -> 5; matrix products, arithmetic and copies ran while one was open for 4% -> 2% of each run, Pallas kernels for 0% -> 0%
where the time goes in v1:
time: 380 us; the launch traced here: 379 us
  waiting for transfers between devices  182 us (48%)
  blocking collectives  85.2 us (22%)
  local copies, waits for them, and re-layouts  52.8 us (14%)
  matrix products  24.1 us (6%)
  between operations  14.3 us (4%)
  starting transfers between devices  13.1 us (3%)
  other arithmetic  7 us (2%)
    all_to_all x1, blocking collectives, local(): received = lax.all_to_all(send_rows, 'req', 0, 0, tiled=True)  70.3 us
    psum x1, waiting for transfers between devices, local(): residual = hidden.astype(jnp.float32) + lax.psum(attn_term, TP)  69.2 us
    reduce_scatter x1, waiting for transfers between devices, local(): partial = lax.psum_scatter(partial, 'tl', scatter_dimension=3, tiled=True)  46.4 us
    all_to_all x1, waiting for transfers between devices, local(): returned = lax.all_to_all(back, ('req', 'th'), 0, 0, tiled=True)  32.4 us
    reduce_scatter x1, waiting for transfers between devices, local(): partial = lax.psum_scatter(partial, 'tc', scatter_dimension=3, tiled=True)  19.7 us
    psum x1, blocking collectives, local(): lax.psum((jnp.sum(query_raw * query_raw, axis=-1), jnp.sum(key_raw * key_...  14.9 us
    all_gather x1, waiting for transfers between devices, local(): rows = lax.all_gather(received, 'tc', axis=2, tiled=True)  14.3 us
    all_to_all x1, starting transfers between devices, local(): returned = lax.all_to_all(back, ('req', 'th'), 0, 0, tiled=True)  12.8 us
  transfers between devices with their start and end apart: 5, of which 5 were waited for; matrix products, arithmetic and copies ran while one was open for 2% of the time, Pallas kernels for 0%

profile of v1, /device:TPU:32, one launch (start us, length us, event | category | flops | bytes accessed | tf_op | source)
XLA Modules:
  0.0 378.7 jit_solution(12945470743647845171)
XLA Ops:
  7.3 1.6 fusion.11
  8.9 4.8 %copy.67 = bf16[2048,3,256]{0,2,1:T(8,128)(2,1)} copy(bf16[2048,3,256]{2,0,1:T(8,128)(2,1)} %param.22) | data formatting | bytes 6291456 | tf_op args[7]
  13.8 3.0 fusion.2
  16.8 0.8 copy-done.6
  21.3 14.9 %all-reduce = (f32[256]{0:T(256)S(1)}, f32[256]{0:T(256)S(1)}) all-reduce(f32[256]{0:T(256)S(1)} %get-tuple-element.3, f32[256]{0:T(256)S(1)} %get-tuple-element.2), channel_id=1, replica_groups=mesh['req'=32,'th'=2,'tl'=2,'tc'=2] {'th','tl','tc'}, use_global_device_ids=true, to_apply=%region_5.0 | all-reduce | flops 512 | bytes 4096 | tf_op jit(solution)/shard_map/psum | solution.py:87
  37.1 0.8 copy.76
  39.0 0.8 copy.70
  39.8 4.9 %gather_fusion = bf16[32,2,128,256]{3,2,1,0:T(8,128)(2,1)} fusion(bf16[2,32,128,256]{3,2,1,0:T(8,128)(2,1)} %param.16, s32[1024]{0:T(1024)S(1)} %pad_clamp_fusion.1), kind=kCustom, calls=%fused_computation | custom fusion | bytes 8388736 | tf_op jit(solution)/shard_map/gather | solution.py:96
  44.7 4.7 %fusion.96 = (bf16[1,32,128,256]{3,2,0,1:T(8,128)(2,1)}, bf16[1,32,128,256]{3,2,0,1:T(8,128)(2,1)}) fusion(bf16[2,32,128,256]{3,2,0,1:T(8,128)(2,1)} %bitcast.107), kind=kLoop, calls=%fused_computation.138 | loop fusion | bytes 8388608 | tf_op jit(solution)/shard_map/slice | solution.py:98
  49.4 2.5 reshape_squeeze.10
  52.0 4.0 %reshape_squeeze.9 = bf16[4,1024,2,128]{3,2,1,0:T(2,128)(2,1)} reshape(bf16[1,32,128,256]{3,2,0,1:T(8,128)(2,1)} %get-tuple-element.11) | data formatting | bytes 4194304 | tf_op jit(solution)/shard_map/reshape;squeeze | solution.py:99
  55.9 1.9 copy.69
  57.8 1.0 fusion.99
  59.8 0.8 fusion.48
  60.8 1.8 fusion.70
  64.3 69.2 %all-reduce.3.cloned.1.call-done = f32[256,2048]{1,0:T(8,128)} async-done(((f32[256,2048]{1,0:T(8,128)}), f32[256,2048]{1,0:T(8,128)}) %all-reduce.3.cloned.1.call-update) | async-done | bytes 2097168 | tf_op jit(solution)/shard_map/psum | solution.py:126
  133.5 1.9 multiply_reduce_fusion
  135.5 1.0 convolution_convert_fusion
  136.5 70.3 %all_to_all.10 = bf16[32,40,1024]{2,1,0:T(8,128)(2,1)} all-to-all(bf16[32,40,1024]{2,1,0:T(8,128)(2,1)S(1)} %convolution_convert_fusion), channel_id=1, replica_groups=mesh['req'=32,'th'=2,'tl'=2,'tc'=2] {'req'}, dimensions={0} | all-to-all | bytes 5242880 | tf_op jit(solution)/shard_map/all_to_all | solution.py:152
  207.1 1.0 copy-done.4
  208.0 1.6 reshape_squeeze.11
  209.6 14.3 %all-gather.2.cloned.1.call-done = bf16[32,40,2048]{2,1,0:T(8,128)(2,1)} async-done(((bf16[32,40,1024]{2,1,0:T(8,128)(2,1)}), bf16[32,40,2048]{2,1,0:T(8,128)(2,1)}) %all-gather.2.cloned.1.call-update) | async-done | bytes 5242896 | tf_op jit(solution)/shard_map/all_gather | solution.py:153
  224.0 5.5 %fusion = f32[32,40,2,256]{3,1,2,0:T(8,128)S(1)} fusion(bf16[32,40,2048]{2,1,0:T(8,128)(2,1)} %all-gather.2.cloned.1.call-done, bf16[2048,2,256]{2,1,0:T(2,128)(2,1)} %bitcast.119), kind=kOutput, calls=%fused_computation.3 | convolution fusion | flops 2684354560 | bytes 9961472 | tf_op jit(solution)/shard_map/scw,wgu->scgu/dot_general | solution.py:154
  229.5 4.0 %convert_bitcast_fusion = bf16[32,2,40,2,2,256]{5,2,3,4,1,0:T(8,128)(2,1)} fusion(bf16[256,2,2,2,256]{4,3,2,1,0:T(2,128)(2,1)S(1)} %copy-done.5, f32[32,40,2,256]{3,1,2,0:T(8,128)S(1)} %fusion), kind=kOutput, calls=%fused_computation.5 | convolution fusion | flops 1346764800 | bytes 8912896 | tf_op jit(solution)/shard_map/scu,uhlkd->shckld/dot_general | solution.py:160
  233.5 10.3 %copy.81 = bf16[32,2,40,2,2,256]{5,4,3,2,1,0:T(2,128)(2,1)} copy(bf16[32,2,40,2,2,256]{5,2,3,4,1,0:T(8,128)(2,1)} %convert_bitcast_fusion) | data formatting | bytes 10485760 | tf_op jit(solution)/shard_map/convert_element_type | solution.py:162
  243.8 9.3 %reshape.284 = bf16[32,2,40,1024]{3,2,1,0:T(8,128)(2,1)} reshape(bf16[32,2,40,2,2,256]{5,4,3,2,1,0:T(2,128)(2,1)} %copy.81) | data formatting | bytes 10485760 | tf_op jit(solution)/shard_map/reshape | solution.py:163
  253.2 19.7 %reduce-scatter.3.cloned.1.call-done = bf16[32,2,40,512]{3,2,1,0:T(8,128)(2,1)} async-done(((bf16[32,2,40,1024]{3,2,1,0:T(8,128)(2,1)}), bf16[32,2,40,512]{3,2,1,0:T(8,128)(2,1)}) %reduce-scatter.3.cloned.1.call-update) | async-done | bytes 2621456 | tf_op jit(solution)/shard_map/reduce_scatter | solution.py:164
  273.0 46.4 %reduce-scatter.5.cloned.1.call-done = bf16[32,2,40,256]{3,2,1,0:T(8,128)(2,1)} async-done(((bf16[32,2,40,512]{3,2,1,0:T(8,128)(2,1)}), bf16[32,2,40,256]{3,2,1,0:T(8,128)(2,1)}) %reduce-scatter.5.cloned.1.call-update) | async-done | bytes 1310736 | tf_op jit(solution)/shard_map/reduce_scatter | solution.py:165
  319.4 12.8 %all-to-all-start.1 = ((bf16[64,40,256]{2,1,0:T(8,128)(2,1)}), bf16[64,40,256]{2,1,0:T(8,128)(2,1)}, u32[]{:S(2)}, u32[]{:S(2)}) async-start(bf16[64,40,256]{2,1,0:T(8,128)(2,1)} %bitcast.108), calls=%async_computation.3 | async-start | bytes 2621440 | tf_op jit(solution)/shard_map/all_to_all | solution.py:167
  332.2 1.0 slice_bitcast_fusion
  335.3 32.4 %all-to-all-done.1 = bf16[64,40,256]{2,1,0:T(8,128)(2,1)} async-done(((bf16[64,40,256]{2,1,0:T(8,128)(2,1)}), bf16[64,40,256]{2,1,0:T(8,128)(2,1)}, u32[]{:S(2)}, u32[]{:S(2)}) %all-to-all-start.1) | async-done | bytes 1310752 | tf_op jit(solution)/shard_map/all_to_all | solution.py:167
  367.7 4.4 %fusion.40 = bf16[256,256]{1,0:T(8,128)(2,1)} fusion(bf16[64,40,256]{2,1,0:T(8,128)(2,1)} %all-to-all-done.1, f32[256,64]{0,1:T(8,128)} %get-tuple-element.4, f32[256,64]{0,1:T(8,128)} %copy-done.9, f32[256,2048]{1,0:T(8,128)S(1)} %get-tuple-element.9, s32[]{:T(128)S(6)} %select_n.47), kind=kOutput, calls=%fused_computation.47 | convolution fusion | flops 2014707712 | bytes 1835012 | tf_op jit(solution)/shard_map/dot_general | solution.py:169
  (104 shorter events, 10.7 us)
Async XLA Ops:
  7.2 53.6 %copy-start = (bf16[256,2048]{1,0:T(8,128)(2,1)S(1)}, bf16[256,2048]{1,0:T(8,128)(2,1)}, u32[]{:S(2)}) copy-start(bf16[256,2048]{1,0:T(8,128)(2,1)} %param.24) | copy-start | bytes 3145732
  7.2 126.3 %all-reduce.3.cloned.1.call-start = ((), (), s32[]{:S(2)}) async-start(), calls=%async_computation.4 | async-start | bytes 4194304 | tf_op jit(solution)/shard_map/psum | solution.py:126
  8.9 4.9 %copy-start.2 = (bf16[256,2048]{1,0:T(8,128)(2,1)S(1)}, bf16[256,2048]{1,0:T(8,128)(2,1)}, u32[]{:S(2)}) copy-start(bf16[256,2048]{1,0:T(8,128)(2,1)} %param.15) | copy-start | bytes 3145732
  8.9 4.9 %copy-start.19 = (f32[2048]{0:T(1024)S(1)}, f32[2048]{0:T(1024)}, u32[]{:S(2)}) copy-start(f32[2048]{0:T(1024)} %param.21) | copy-start | bytes 24580
  13.7 4.0 %copy-start.15 = (s32[4,8]{1,0:T(4,128)S(1)}, s32[4,8]{1,0:T(4,128)}, u32[]{:S(2)}) copy-start(s32[4,8]{1,0:T(4,128)} %param.17) | copy-start | bytes 388
  13.7 4.1 %copy-start.16 = (s32[4,8]{1,0:T(4,128)S(1)}, s32[4,8]{1,0:T(4,128)}, u32[]{:S(2)}) copy-start(s32[4,8]{1,0:T(4,128)} %param.20) | copy-start | bytes 388
  13.7 4.2 %copy-start.17 = (f32[2,256]{1,0:T(2,128)S(1)}, f32[2,256]{1,0:T(2,128)}, u32[]{:S(2)}) copy-start(f32[2,256]{1,0:T(2,128)} %param.23) | copy-start | bytes 6148
  13.8 4.3 %copy-start.14 = (s32[4]{0:T(128)S(1)}, s32[4]{0:T(128)}, u32[]{:S(2)}) copy-start(s32[4]{0:T(128)} %param.18) | copy-start | bytes 52
  13.8 4.3 %copy-start.18 = (s32[4,64]{1,0:T(4,128)S(1)}, s32[4,64]{1,0:T(4,128)}, u32[]{:S(2)}) copy-start(s32[4,64]{1,0:T(4,128)} %param.19) | copy-start | bytes 3076
  16.8 0.9 copy-start.6
  57.8 1.0 copy-start.7
  57.8 1.0 copy-start.8
  57.8 1.0 copy-start.11
  58.9 0.9 copy-start.10
  60.8 1.9 copy-start.12
  60.8 1.9 copy-start.13
  62.5 71.0 %copy-start.3 = (bf16[256,2048]{1,0:T(8,128)(2,1)S(1)}, bf16[256,2048]{1,0:T(8,128)(2,1)}, u32[]{:S(2)}) copy-start(bf16[256,2048]{1,0:T(8,128)(2,1)} %param.15) | copy-start | bytes 3145732
  62.6 161.4 %all-gather.2.cloned.1.call-start = ((), (), s32[]{:S(2)}) async-start(), calls=%async_computation.5 | async-start | bytes 7864320 | tf_op jit(solution)/shard_map/all_gather | solution.py:153
  63.6 0.6 copy-start.9
  64.3 71.2 %dynamic-slice-start = ((f32[2048]{0:T(1024)}, s32[]{:T(128)}), f32[1024]{0:T(1024)S(1)}, s32[]{:S(2)}) async-start(f32[2048]{0:T(1024)} %param.25, s32[]{:T(128)} %select_n.50), calls=%async_computation.8 | async-start | bytes 8704 | tf_op jit(solution)/shard_map/dynamic_slice | solution.py:148
  206.8 1.2 copy-start.4
  206.8 66.1 %reduce-scatter.3.cloned.1.call-start = ((), (), s32[]{:S(2)}) async-start(), calls=%async_computation.6 | async-start | bytes 7864320 | tf_op jit(solution)/shard_map/reduce_scatter | solution.py:164
  224.0 5.5 %copy-start.5 = (bf16[256,2,2,2,256]{4,3,2,1,0:T(2,128)(2,1)S(1)}, bf16[256,2,2,2,256]{4,3,2,1,0:T(2,128)(2,1)}, u32[]{:S(2)}) copy-start(bf16[256,2,2,2,256]{4,3,2,1,0:T(2,128)(2,1)} %reshape_squeeze.11) | copy-start | bytes 3145732
  253.2 66.2 %reduce-scatter.5.cloned.1.call-start = ((), (), s32[]{:S(2)}) async-start(), calls=%async_computation.7 | async-start | bytes 3932160 | tf_op jit(solution)/shard_map/reduce_scatter | solution.py:165
  319.4 48.3 %all-to-all-start.1 = ((bf16[64,40,256]{2,1,0:T(8,128)(2,1)}), bf16[64,40,256]{2,1,0:T(8,128)(2,1)}, u32[]{:S(2)}, u32[]{:S(2)}) async-start(bf16[64,40,256]{2,1,0:T(8,128)(2,1)} %bitcast.108), calls=%async_computation.3 | async-start | bytes 2621440 | tf_op jit(solution)/shard_map/all_to_all | solution.py:167
  367.7 4.4 %copy-start.1 = (bf16[256,2048]{1,0:T(8,128)(2,1)S(1)}, bf16[256,2048]{1,0:T(8,128)(2,1)}, u32[]{:S(2)}) copy-start(bf16[256,2048]{1,0:T(8,128)(2,1)} %param.24) | copy-start | bytes 3145732
Sparse Core Ops, SparseCore 0:
  62.7 70.7 all-reduce.2
  206.9 16.9 all-gather.1
  253.3 19.5 reduce-scatter.2
  275.3 44.0 reduce-scatter.4

commit v2 on v1

--- a/solution.py
+++ b/solution.py
@@ -150,20 +150,39 @@
         "ict,tw->icw", select, normed_half, preferred_element_type=jnp.float32
     ).astype(jnp.bfloat16)
     received = lax.all_to_all(send_rows, "req", 0, 0, tiled=True)
-    rows = lax.all_gather(received, "tc", axis=2, tiled=True)
+    partner_rows = lax.ppermute(received, "tc", [(0, 1), (1, 0)])
+    own_weights = lax.dynamic_slice_in_dim(w_gate_up[0], tc * half_width, half_width, 0)
+    partner_weights = lax.dynamic_slice_in_dim(w_gate_up[0], (1 - tc) * half_width, half_width, 0)
     gate_up = jnp.einsum(
-        "scw,wgu->scgu", rows, w_gate_up[0], preferred_element_type=jnp.float32
+        "scw,wgu->scgu", received, own_weights, preferred_element_type=jnp.float32
+    ) + jnp.einsum(
+        "scw,wgu->scgu", partner_rows, partner_weights, preferred_element_type=jnp.float32
     )
     activated = (jax.nn.silu(gate_up[..., 0, :]) * gate_up[..., 1, :]).astype(jnp.bfloat16)
     units_dev = w_down.shape[1]
-    down = w_down[0].reshape(units_dev, 2, 2, 2, slice_width)
+    down = (
+        w_down[0]
+        .reshape(units_dev, 2, 2, 2, slice_width)
+        .transpose(0, 3, 2, 1, 4)
+        .reshape(units_dev, model_width)
+    )
     partial = jnp.einsum(
-        "scu,uhlkd->shckld", activated, down, preferred_element_type=jnp.float32
+        "scu,uw->scw", activated, down, preferred_element_type=jnp.float32
     ).astype(jnp.bfloat16)
-    partial = partial.reshape(req_count, 2, capacity, 4 * slice_width)
-    partial = lax.psum_scatter(partial, "tc", scatter_dimension=3, tiled=True)
-    partial = lax.psum_scatter(partial, "tl", scatter_dimension=3, tiled=True)
-    back = partial.reshape(req_count * 2, capacity, slice_width)
+    swap = [(0, 1), (1, 0)]
+    half = model_width // 2
+    kept = lax.dynamic_slice_in_dim(partial, tc * half, half, 2)
+    given = lax.dynamic_slice_in_dim(partial, (1 - tc) * half, half, 2)
+    pair_sum = kept.astype(jnp.float32) + lax.ppermute(given, "tc", swap).astype(jnp.float32)
+    quarter = half // 2
+    kept = lax.dynamic_slice_in_dim(pair_sum, tl * quarter, quarter, 2)
+    given = lax.dynamic_slice_in_dim(pair_sum, (1 - tl) * quarter, quarter, 2).astype(jnp.bfloat16)
+    quad_sum = (kept + lax.ppermute(given, "tl", swap).astype(jnp.float32)).astype(jnp.bfloat16)
+    back = (
+        quad_sum.reshape(req_count, capacity, 2, slice_width)
+        .transpose(0, 2, 1, 3)
+        .reshape(req_count * 2, capacity, slice_width)
+    )
     returned = lax.all_to_all(back, ("req", "th"), 0, 0, tiled=True)
     combine = weight_of[:, :, None] * (slot_of[:, :, None] == cap_ids[None, None, :])
     mixture = jnp.dot(

time: 380 us -> 326 us (0.86)
  waiting for transfers between devices: 182 us -> 139 us
  local copies, waits for them, and re-layouts: 52.8 us -> 41.6 us
  other arithmetic: 7 us -> 13.9 us
  starting transfers between devices: 13.1 us -> 8.41 us
    reduce_scatter x2 -> x0, waiting for transfers between devices: 66.1 us -> none  [the longest x1 46.4 us: local(): partial = lax.psum_scatter(partial, 'tl', scatter_dimension=3, tiled=True)]
    ppermute x0 -> x3, waiting for transfers between devices: none -> 36 us  [the longest x1 31.1 us: local(): lax.ppermute(given, 'tl', swap).astype(jnp.float32)]
    all_gather x1 -> x0, waiting for transfers between devices: 14.3 us -> none  [local(): rows = lax.all_gather(received, 'tc', axis=2, tiled=True)]
    convert_element_type x1, local copies, waits for them, and re-layouts: 10.3 us -> 0.2 us  [local(): lax.dynamic_slice_in_dim(pair_sum, (1 - tl) * quarter, quarter, 2)]
    reshape x1, local copies, waits for them, and re-layouts: 9.35 us -> 0.82 us  [local(): down = w_down[0].reshape(units_dev, 2, 2, 2, slice_width).transpose(0, 3,...]
    dynamic_slice x0 -> x2, local copies, waits for them, and re-layouts: none -> 5.03 us  [the longest x1 2.99 us: local(): lax.dynamic_slice_in_dim(w_gate_up[0], (1 - tc) * half_width, half_width, 0)]
    all_to_all x1, starting transfers between devices: 12.8 us -> 7.78 us  [local(): returned = lax.all_to_all(back, ('req', 'th'), 0, 0, tiled=True)]
    unnamed x43 -> x45, local copies, waits for them, and re-layouts: 7.29 us -> 9.26 us
  transfers between devices with their start and end apart: 5 -> 5, of which waited for: 5 -> 4; matrix products, arithmetic and copies ran while one was open for 2% -> 4% of each run, Pallas kernels for 0% -> 0%
where the time goes in v2:
time: 326 us; the launch traced here: 325 us
  waiting for transfers between devices  139 us (43%)
  blocking collectives  85.3 us (26%)
  local copies, waits for them, and re-layouts  41.6 us (13%)
  matrix products  22.4 us (7%)
  between operations  14.7 us (5%)
  other arithmetic  13.9 us (4%)
  starting transfers between devices  8.41 us (3%)
    all_to_all x1, blocking collectives, local(): received = lax.all_to_all(send_rows, 'req', 0, 0, tiled=True)  70.4 us
    psum x1, waiting for transfers between devices, local(): residual = hidden.astype(jnp.float32) + lax.psum(attn_term, TP)  70.4 us
    all_to_all x1, waiting for transfers between devices, local(): returned = lax.all_to_all(back, ('req', 'th'), 0, 0, tiled=True)  32.5 us
    ppermute x1, waiting for transfers between devices, local(): lax.ppermute(given, 'tl', swap).astype(jnp.float32)  31.1 us
    psum x1, blocking collectives, local(): lax.psum((jnp.sum(query_raw * query_raw, axis=-1), jnp.sum(key_raw * key_...  14.9 us
    unnamed x45, local copies, waits for them, and re-layouts  9.26 us
    all_to_all x1, starting transfers between devices, local(): returned = lax.all_to_all(back, ('req', 'th'), 0, 0, tiled=True)  7.78 us
  transfers between devices with their start and end apart: 5, of which 4 were waited for; matrix products, arithmetic and copies ran while one was open for 4% of the time, Pallas kernels for 0%

profile of v2, /device:TPU:32, one launch (start us, length us, event | category | flops | bytes accessed | tf_op | source)
XLA Modules:
  0.0 325.3 jit_solution(18216721312745259768)
XLA Ops:
  7.3 1.6 fusion.13
  8.9 4.8 %copy.88 = bf16[2048,3,256]{0,2,1:T(8,128)(2,1)} copy(bf16[2048,3,256]{2,0,1:T(8,128)(2,1)} %param.22) | data formatting | bytes 6291456 | tf_op args[7]
  13.7 3.0 fusion
  21.3 14.9 %all-reduce = (f32[256]{0:T(256)S(1)}, f32[256]{0:T(256)S(1)}) all-reduce(f32[256]{0:T(256)S(1)} %get-tuple-element.3, f32[256]{0:T(256)S(1)} %get-tuple-element.2), channel_id=1, replica_groups=mesh['req'=32,'th'=2,'tl'=2,'tc'=2] {'th','tl','tc'}, use_global_device_ids=true, to_apply=%region_5.0 | all-reduce | flops 512 | bytes 4096 | tf_op jit(solution)/shard_map/psum | solution.py:87
  39.8 4.9 %gather_fusion = bf16[32,2,128,256]{3,2,1,0:T(8,128)(2,1)} fusion(bf16[2,32,128,256]{3,2,1,0:T(8,128)(2,1)} %param.16, s32[1024]{0:T(1024)S(1)} %pad_clamp_fusion.1), kind=kCustom, calls=%fused_computation | custom fusion | bytes 8388736 | tf_op jit(solution)/shard_map/gather | solution.py:96
  44.8 4.7 %fusion.101 = (bf16[1,32,128,256]{3,2,0,1:T(8,128)(2,1)}, bf16[1,32,128,256]{3,2,0,1:T(8,128)(2,1)}) fusion(bf16[2,32,128,256]{3,2,0,1:T(8,128)(2,1)} %bitcast.111), kind=kLoop, calls=%fused_computation.148 | loop fusion | bytes 8388608 | tf_op jit(solution)/shard_map/slice | solution.py:98
  49.5 2.5 reshape_squeeze.10
  52.0 4.0 %reshape_squeeze.9 = bf16[4,1024,2,128]{3,2,1,0:T(2,128)(2,1)} reshape(bf16[1,32,128,256]{3,2,0,1:T(8,128)(2,1)} %get-tuple-element.11) | data formatting | bytes 4194304 | tf_op jit(solution)/shard_map/reshape;squeeze | solution.py:99
  56.0 1.9 copy.90
  57.9 1.0 fusion.105
  60.9 1.8 fusion.75
  63.2 70.4 %all-reduce.3.cloned.1.call-done = f32[256,2048]{1,0:T(8,128)} async-done(((f32[256,2048]{1,0:T(8,128)}), f32[256,2048]{1,0:T(8,128)}) %all-reduce.3.cloned.1.call-update) | async-done | bytes 2097168 | tf_op jit(solution)/shard_map/psum | solution.py:126
  133.6 1.9 multiply_reduce_fusion
  135.6 1.0 convolution_convert_fusion.1
  136.6 70.4 %all_to_all.10 = bf16[32,40,1024]{2,1,0:T(8,128)(2,1)} all-to-all(bf16[32,40,1024]{2,1,0:T(8,128)(2,1)S(1)} %convolution_convert_fusion.1), channel_id=1, replica_groups=mesh['req'=32,'th'=2,'tl'=2,'tc'=2] {'req'}, dimensions={0} | all-to-all | bytes 5242880 | tf_op jit(solution)/shard_map/all_to_all | solution.py:152
  207.8 1.1 copy.102
  209.8 3.0 constant_dynamic-slice_fusion.1
  212.7 3.3 %fusion.4 = f32[32,40,2,256]{3,1,2,0:T(8,128)S(1)} fusion(bf16[32,40,1024]{2,1,0:T(8,128)(2,1)} %all_to_all.10, bf16[1,1024,2,256]{3,2,1,0:T(2,128)(2,1)S(1)} %get-tuple-element.13), kind=kOutput, calls=%fused_computation.12 | convolution fusion | flops 1342177280 | bytes 6291456 | tf_op jit(solution)/shard_map/scw,wgu->scgu/dot_general | solution.py:156
  216.1 3.4 %fusion.21 = f32[32,40,2,256]{3,1,2,0:T(8,128)S(1)} fusion(f32[32,40,2,256]{3,1,2,0:T(8,128)S(1)} %fusion.4, bf16[32,40,1024]{2,1,0:T(8,128)(2,1)} %collective-permute-done, bf16[1,1024,2,256]{3,2,1,0:T(2,128)(2,1)S(1)} %get-tuple-element.12), kind=kOutput, calls=%fused_computation.35 | convolution fusion | flops 1342832640 | bytes 8912896 | tf_op jit(solution)/shard_map/scw,wgu->scgu/dot_general | solution.py:158
  219.4 1.6 convolution_convert_fusion
  221.1 2.0 constant_dynamic-slice_fusion
  223.1 1.2 copy-done.3
  224.8 4.9 %collective-permute-done.1 = bf16[32,40,1024]{2,1,0:T(8,128)(2,1)} collective-permute-done((bf16[32,40,1024]{2,1,0:T(8,128)(2,1)}, bf16[32,40,1024]{2,1,0:T(8,128)(2,1)}, u32[]{:S(2)}, u32[]{:S(2)}) %collective-permute-start.1) | collective-permute-done | bytes 2621472 | tf_op jit(solution)/shard_map/ppermute | solution.py:176
  229.7 3.7 %convert_add_fusion = f32[32,40,1024]{2,1,0:T(8,128)S(1)} fusion(bf16[32,40,1024]{2,1,0:T(8,128)(2,1)} %collective-permute-done.1, bf16[32,40,2048]{2,1,0:T(8,128)(2,1)} %copy-done.3, s32[]{:T(128)} %select_n.62), kind=kLoop, calls=%fused_computation.3 | loop fusion | flops 3932160 | bytes 10485764 | tf_op jit(solution)/shard_map/add | solution.py:176
  233.4 2.3 copy-done.2
  236.0 31.1 %collective-permute-done.2 = bf16[32,40,512]{2,1,0:T(8,128)(2,1)} collective-permute-done((bf16[32,40,512]{2,1,0:T(8,128)(2,1)S(1)}, bf16[32,40,512]{2,1,0:T(8,128)(2,1)}, u32[]{:S(2)}, u32[]{:S(2)}) %collective-permute-start.2) | collective-permute-done | bytes 1310752 | tf_op jit(solution)/shard_map/ppermute | solution.py:180
  267.1 2.6 add_convert_fusion
  269.8 1.2 pad_maximum_fusion
  271.0 7.8 %all-to-all-start.1 = ((bf16[64,40,256]{2,1,0:T(8,128)(2,1)}), bf16[64,40,256]{2,1,0:T(8,128)(2,1)S(1)}, u32[]{:S(2)}, u32[]{:S(2)}) async-start(bf16[64,40,256]{2,1,0:T(8,128)(2,1)} %bitcast.24), calls=%async_computation.1 | async-start | bytes 2621440 | tf_op jit(solution)/shard_map/all_to_all | solution.py:186
  278.8 1.0 slice_bitcast_fusion
  281.9 32.5 %all-to-all-done.1 = bf16[64,40,256]{2,1,0:T(8,128)(2,1)S(1)} async-done(((bf16[64,40,256]{2,1,0:T(8,128)(2,1)}), bf16[64,40,256]{2,1,0:T(8,128)(2,1)S(1)}, u32[]{:S(2)}, u32[]{:S(2)}) %all-to-all-start.1) | async-done | bytes 1310752 | tf_op jit(solution)/shard_map/all_to_all | solution.py:186
  314.4 4.0 %fusion.43 = bf16[256,256]{1,0:T(8,128)(2,1)} fusion(bf16[64,40,256]{2,1,0:T(8,128)(2,1)S(1)} %all-to-all-done.1, f32[256,64]{0,1:T(8,128)S(1)} %get-tuple-element.4, f32[256,64]{0,1:T(8,128)S(1)} %fusion.74, f32[256,2048]{1,0:T(8,128)} %copy-done.6, s32[]{:T(128)S(6)} %select_n.59), kind=kOutput, calls=%fused_computation.52 | convolution fusion | flops 2014707712 | bytes 1835012 | tf_op jit(solution)/shard_map/dot_general | solution.py:188
  (111 shorter events, 15.1 us)
Async XLA Ops:
  7.2 53.7 %copy-start = (bf16[256,2048]{1,0:T(8,128)(2,1)S(1)}, bf16[256,2048]{1,0:T(8,128)(2,1)}, u32[]{:S(2)}) copy-start(bf16[256,2048]{1,0:T(8,128)(2,1)} %param.24) | copy-start | bytes 3145732
  7.2 126.4 %all-reduce.3.cloned.1.call-start = ((), (), s32[]{:S(2)}) async-start(), calls=%async_computation.2 | async-start | bytes 4194304 | tf_op jit(solution)/shard_map/psum | solution.py:126
  8.9 4.8 %copy-start.4 = (bf16[256,2048]{1,0:T(8,128)(2,1)S(1)}, bf16[256,2048]{1,0:T(8,128)(2,1)}, u32[]{:S(2)}) copy-start(bf16[256,2048]{1,0:T(8,128)(2,1)} %param.15) | copy-start | bytes 3145732
  8.9 4.8 %copy-start.20 = (f32[2048]{0:T(1024)S(1)}, f32[2048]{0:T(1024)}, u32[]{:S(2)}) copy-start(f32[2048]{0:T(1024)} %param.21) | copy-start | bytes 24580
  13.7 4.1 %copy-start.16 = (s32[4,8]{1,0:T(4,128)S(1)}, s32[4,8]{1,0:T(4,128)}, u32[]{:S(2)}) copy-start(s32[4,8]{1,0:T(4,128)} %param.17) | copy-start | bytes 388
  13.7 4.2 %copy-start.17 = (s32[4,8]{1,0:T(4,128)S(1)}, s32[4,8]{1,0:T(4,128)}, u32[]{:S(2)}) copy-start(s32[4,8]{1,0:T(4,128)} %param.20) | copy-start | bytes 388
  13.7 4.3 %copy-start.18 = (f32[2,256]{1,0:T(2,128)S(1)}, f32[2,256]{1,0:T(2,128)}, u32[]{:S(2)}) copy-start(f32[2,256]{1,0:T(2,128)} %param.23) | copy-start | bytes 6148
  13.7 4.3 %copy-start.15 = (s32[4]{0:T(128)S(1)}, s32[4]{0:T(128)}, u32[]{:S(2)}) copy-start(s32[4]{0:T(128)} %param.18) | copy-start | bytes 52
  13.7 4.4 %copy-start.19 = (s32[4,64]{1,0:T(4,128)S(1)}, s32[4,64]{1,0:T(4,128)}, u32[]{:S(2)}) copy-start(s32[4,64]{1,0:T(4,128)} %param.19) | copy-start | bytes 3076
  16.7 0.9 copy-start.8
  57.9 1.0 copy-start.9
  57.9 1.0 copy-start.10
  57.9 1.0 copy-start.12
  58.9 0.9 copy-start.11
  60.8 1.8 copy-start.13
  60.8 1.8 copy-start.14
  62.6 71.0 %copy-start.5 = (bf16[256,2048]{1,0:T(8,128)(2,1)S(1)}, bf16[256,2048]{1,0:T(8,128)(2,1)}, u32[]{:S(2)}) copy-start(bf16[256,2048]{1,0:T(8,128)(2,1)} %param.15) | copy-start | bytes 3145732
  63.2 72.4 %dynamic-slice-start = ((f32[2048]{0:T(1024)}, s32[]{:T(128)}), f32[1024]{0:T(1024)S(1)}, s32[]{:S(2)}) async-start(f32[2048]{0:T(1024)} %param.25, s32[]{:T(128)} %select_n.62), calls=%async_computation.3 | async-start | bytes 8704 | tf_op jit(solution)/shard_map/dynamic_slice | solution.py:148
  135.5 71.5 %copy-start.6 = (f32[256,2048]{1,0:T(8,128)}, f32[256,2048]{1,0:T(8,128)S(1)}, u32[]{:S(2)}) copy-start(f32[256,2048]{1,0:T(8,128)S(1)} %get-tuple-element.9) | copy-start | bytes 6291460
  136.6 70.5 %copy-start.7 = (bf16[1,256,2048]{2,1,0:T(8,128)(2,1)S(1)}, bf16[1,256,2048]{2,1,0:T(8,128)(2,1)}, u32[]{:S(2)}) copy-start(bf16[1,256,2048]{2,1,0:T(8,128)(2,1)} %param.29) | copy-start | bytes 3145732
  207.0 9.0 %collective-permute-start = (bf16[32,40,1024]{2,1,0:T(8,128)(2,1)}, bf16[32,40,1024]{2,1,0:T(8,128)(2,1)}, u32[]{:S(2)}, u32[]{:S(2)}) collective-permute-start(bf16[32,40,1024]{2,1,0:T(8,128)(2,1)} %all_to_all.10), channel_id=1, source_target_pairs={{0,1},{1,0},{2,3},{3,2},{4,5},{5,4},{6,7},{7,6},{8,9},{9,8},{10,11... | collective-permute-start | bytes 7864328 | tf_op jit(solution)/shard_map/ppermute | solution.py:153
  221.1 3.2 copy-start.3
  224.3 5.4 %collective-permute-start.1 = (bf16[32,40,1024]{2,1,0:T(8,128)(2,1)}, bf16[32,40,1024]{2,1,0:T(8,128)(2,1)}, u32[]{:S(2)}, u32[]{:S(2)}) collective-permute-start(bf16[32,40,1024]{2,1,0:T(8,128)(2,1)} %constant_dynamic-slice_fusion), channel_id=1, source_target_pairs={{0,1},{1,0},{2,3},{3,2},{4,5},{5,4},{6,7},{7,6},{8,9},{9,8},{10,11... | collective-permute-start | bytes 7864328 | tf_op jit(solution)/shard_map/ppermute | solution.py:176
  233.4 2.3 copy-start.2
  235.9 31.2 %collective-permute-start.2 = (bf16[32,40,512]{2,1,0:T(8,128)(2,1)S(1)}, bf16[32,40,512]{2,1,0:T(8,128)(2,1)}, u32[]{:S(2)}, u32[]{:S(2)}) collective-permute-start(bf16[32,40,512]{2,1,0:T(8,128)(2,1)S(1)} %dynamic-slice_convert_fusion), channel_id=1, source_target_pairs={{0,2},{2,0},{1,3},{3,1},{4,6},{6,4},{5,7},{7,5},{8,10},{10,8},{9,1... | collective-permute-start | bytes 3932168 | tf_op jit(solution)/shard_map/ppermute | solution.py:180
  271.0 43.4 %all-to-all-start.1 = ((bf16[64,40,256]{2,1,0:T(8,128)(2,1)}), bf16[64,40,256]{2,1,0:T(8,128)(2,1)S(1)}, u32[]{:S(2)}, u32[]{:S(2)}) async-start(bf16[64,40,256]{2,1,0:T(8,128)(2,1)} %bitcast.24), calls=%async_computation.1 | async-start | bytes 2621440 | tf_op jit(solution)/shard_map/all_to_all | solution.py:186
  314.4 4.0 %copy-start.1 = (bf16[256,2048]{1,0:T(8,128)(2,1)S(1)}, bf16[256,2048]{1,0:T(8,128)(2,1)}, u32[]{:S(2)}) copy-start(bf16[256,2048]{1,0:T(8,128)(2,1)} %param.24) | copy-start | bytes 3145732
Sparse Core Ops, SparseCore 0:
  62.8 70.7 all-reduce.2

commit v3 on v2

--- a/solution.py
+++ b/solution.py
@@ -123,10 +123,29 @@
         .reshape(tok_rows, feat_dev)
     )
     attn_term = jnp.dot(attn_heads, w_out, preferred_element_type=jnp.float32)
-    residual = hidden.astype(jnp.float32) + lax.psum(attn_term, TP)
-    normed_moe = rms_scale(residual, moe_gain).astype(jnp.bfloat16)
-    residual_share = lax.dynamic_slice_in_dim(residual, slice_start, slice_width, 1)
+    swap = [(0, 1), (1, 0)]
+    column_groups = model_width // (2 * slice_width)
+    attn_blocks = attn_term.reshape(tok_rows, column_groups, 2, slice_width)
+    kept = lax.dynamic_index_in_dim(attn_blocks, tc, axis=2, keepdims=False)
+    given = lax.dynamic_index_in_dim(attn_blocks, 1 - tc, axis=2, keepdims=False)
+    chip_sum = kept + lax.ppermute(given, "tc", swap)
+    hidden_blocks = hidden.astype(jnp.float32).reshape(tok_rows, column_groups, 2, slice_width)
+    residual = lax.dynamic_index_in_dim(hidden_blocks, tc, axis=2, keepdims=False) + lax.psum(
+        chip_sum, ("th", "tl")
+    )
+    own_squares = jnp.sum(residual * residual, axis=(1, 2))
+    all_squares = own_squares + lax.ppermute(own_squares, "tc", swap)
+    gain_here = lax.dynamic_index_in_dim(
+        moe_gain.reshape(column_groups, 2, slice_width), tc, axis=1, keepdims=False
+    )
+    normed_half = (
+        residual * lax.rsqrt(all_squares / model_width + norm_eps)[:, None, None] * gain_here
+    ).astype(jnp.bfloat16).reshape(tok_rows, column_groups * slice_width)
+    residual_share = lax.dynamic_index_in_dim(
+        residual, th * lax.axis_size("tl") + tl, axis=1, keepdims=False
+    )
     experts_here = EXPERTS // req_count
+    units_dev = w_down.shape[1]
     tok_ids = jnp.arange(tok_rows, dtype=jnp.int32)
     route_hot = (routes[:, :, None] == jnp.arange(EXPERTS, dtype=jnp.int32)).astype(jnp.float32)
     per_token = jnp.sum(route_hot, axis=1)
@@ -144,22 +163,24 @@
     select = jnp.where(
         (picked_here[:, None, :] > 0.5) & (slot_here[:, None, :] == cap_ids[None, :, None]), 1.0, 0.0
     ).astype(jnp.bfloat16)
-    half_width = model_width // 2
-    normed_half = lax.dynamic_slice_in_dim(normed_moe, tc * half_width, half_width, 1)
     send_rows = jnp.einsum(
         "ict,tw->icw", select, normed_half, preferred_element_type=jnp.float32
     ).astype(jnp.bfloat16)
     received = lax.all_to_all(send_rows, "req", 0, 0, tiled=True)
     partner_rows = lax.ppermute(received, "tc", [(0, 1), (1, 0)])
-    own_weights = lax.dynamic_slice_in_dim(w_gate_up[0], tc * half_width, half_width, 0)
-    partner_weights = lax.dynamic_slice_in_dim(w_gate_up[0], (1 - tc) * half_width, half_width, 0)
+    weight_blocks = w_gate_up[0].reshape(column_groups, 2, slice_width, 2, units_dev)
+    own_weights = lax.dynamic_index_in_dim(weight_blocks, tc, axis=1, keepdims=False).reshape(
+        model_width // 2, 2, units_dev
+    )
+    partner_weights = lax.dynamic_index_in_dim(
+        weight_blocks, 1 - tc, axis=1, keepdims=False
+    ).reshape(model_width // 2, 2, units_dev)
     gate_up = jnp.einsum(
         "scw,wgu->scgu", received, own_weights, preferred_element_type=jnp.float32
     ) + jnp.einsum(
         "scw,wgu->scgu", partner_rows, partner_weights, preferred_element_type=jnp.float32
     )
     activated = (jax.nn.silu(gate_up[..., 0, :]) * gate_up[..., 1, :]).astype(jnp.bfloat16)
-    units_dev = w_down.shape[1]
     down = (
         w_down[0]
         .reshape(units_dev, 2, 2, 2, slice_width)

time: 326 us -> 318 us (0.975)
  waiting for transfers between devices: 139 us -> 119 us
  local copies, waits for them, and re-layouts: 41.6 us -> 49.2 us
    psum x1, waiting for transfers between devices: 70.4 us -> 47.2 us  [local(): lax.psum(chip_sum, ('th', 'tl'))]
    ppermute x0 -> x2, waiting for transfers between devices: none -> 4.09 us  [the longest x1 3 us: local(): chip_sum = kept + lax.ppermute(given, 'tc', swap)]
    unnamed x45 -> x46, local copies, waits for them, and re-layouts: 9.26 us -> 10.5 us
  transfers between devices with their start and end apart: 5 -> 7, of which waited for: 4 -> 6; matrix products, arithmetic and copies ran while one was open for 4% -> 6% of each run, Pallas kernels for 0% -> 0%
where the time goes in v3:
time: 318 us
  waiting for transfers between devices  119 us (37%)
  blocking collectives  87.4 us (27%)
  local copies, waits for them, and re-layouts  49.2 us (15%)
  matrix products  21.5 us (7%)
  other arithmetic  16.5 us (5%)
  between operations  14.7 us (5%)
  starting transfers between devices  9.39 us (3%)
    all_to_all x1, blocking collectives, local(): received = lax.all_to_all(send_rows, 'req', 0, 0, tiled=True)  72.6 us
    psum x1, waiting for transfers between devices, local(): lax.psum(chip_sum, ('th', 'tl'))  47.2 us
    all_to_all x1, waiting for transfers between devices, local(): returned = lax.all_to_all(back, ('req', 'th'), 0, 0, tiled=True)  32.3 us
    ppermute x1, waiting for transfers between devices, local(): lax.ppermute(given, 'tl', swap).astype(jnp.float32)  30.3 us
    psum x1, blocking collectives, local(): lax.psum((jnp.sum(query_raw * query_raw, axis=-1), jnp.sum(key_raw * key_...  14.9 us
    unnamed x46, local copies, waits for them, and re-layouts  10.5 us
    all_to_all x1, starting transfers between devices, local(): returned = lax.all_to_all(back, ('req', 'th'), 0, 0, tiled=True)  7.84 us
  transfers between devices with their start and end apart: 7, of which 6 were waited for; matrix products, arithmetic and copies ran while one was open for 6% of the time, Pallas kernels for 0%

profile of v3, /device:TPU:32, one launch (start us, length us, event | category | flops | bytes accessed | tf_op | source)
XLA Modules:
  0.0 317.6 jit_solution(13410904621526826133)
XLA Ops:
  7.3 1.5 multiply_reduce_fusion
  8.8 4.8 %copy.101 = bf16[2048,3,256]{0,2,1:T(8,128)(2,1)} copy(bf16[2048,3,256]{2,0,1:T(8,128)(2,1)} %param.22) | data formatting | bytes 6291456 | tf_op args[7]
  13.7 3.0 fusion
  20.9 1.3 copy.128
  22.5 14.9 %all-reduce = (f32[256]{0:T(256)S(1)}, f32[256]{0:T(256)S(1)}) all-reduce(f32[256]{0:T(256)S(1)} %get-tuple-element.3, f32[256]{0:T(256)S(1)} %get-tuple-element.2), channel_id=1, replica_groups=mesh['req'=32,'th'=2,'tl'=2,'tc'=2] {'th','tl','tc'}, use_global_device_ids=true, to_apply=%region_5.0 | all-reduce | flops 512 | bytes 4096 | tf_op jit(solution)/shard_map/psum | solution.py:87
  41.1 4.9 %gather_fusion = bf16[32,2,128,256]{3,2,1,0:T(8,128)(2,1)} fusion(bf16[2,32,128,256]{3,2,1,0:T(8,128)(2,1)} %param.16, s32[1024]{0:T(1024)S(1)} %pad_clamp_fusion.1), kind=kCustom, calls=%fused_computation | custom fusion | bytes 8388736 | tf_op jit(solution)/shard_map/gather | solution.py:96
  46.0 4.7 %fusion.82 = (bf16[1,32,128,256]{3,2,0,1:T(8,128)(2,1)}, bf16[1,32,128,256]{3,2,0,1:T(8,128)(2,1)}) fusion(bf16[2,32,128,256]{3,2,0,1:T(8,128)(2,1)} %bitcast.122), kind=kLoop, calls=%fused_computation.140 | loop fusion | bytes 8388608 | tf_op jit(solution)/shard_map/slice | solution.py:98
  50.7 2.5 reshape_squeeze.13
  53.3 4.0 %reshape_squeeze.12 = bf16[4,1024,2,128]{3,2,1,0:T(2,128)(2,1)} reshape(bf16[1,32,128,256]{3,2,0,1:T(8,128)(2,1)} %get-tuple-element.11) | data formatting | bytes 4194304 | tf_op jit(solution)/shard_map/reshape;squeeze | solution.py:99
  57.3 1.9 copy.103
  62.2 1.7 fusion.57
  65.0 3.0 collective-permute-done
  68.0 2.4 bitcast_add_fusion
  70.4 2.1 reshape.293
  74.6 47.2 %all-reduce.3.cloned.1.call-done = f32[256,4,256]{2,0,1:T(8,128)} async-done(((f32[256,4,256]{2,0,1:T(8,128)}), f32[256,4,256]{2,0,1:T(8,128)}) %all-reduce.3.cloned.1.call-update) | async-done | bytes 1048592 | tf_op jit(solution)/shard_map/psum | solution.py:133
  121.8 1.5 multiply_reduce_fusion.1
  126.4 72.6 %all_to_all.10 = bf16[32,40,1024]{2,1,0:T(8,128)(2,1)} all-to-all(bf16[32,40,1024]{2,1,0:T(8,128)(2,1)S(1)} %convolution_convert_fusion.1), channel_id=1, replica_groups=mesh['req'=32,'th'=2,'tl'=2,'tc'=2] {'req'}, dimensions={0} | all-to-all | bytes 5242880 | tf_op jit(solution)/shard_map/all_to_all | solution.py:169
  201.7 3.0 constant_dynamic-slice_fusion.1
  206.0 3.6 %fusion.4 = f32[32,40,2,256]{3,1,2,0:T(8,128)S(1)} fusion(bf16[1024,2,256,1]{2,0,1,3:T(8,128)(2,1)} %bitcast.128, bf16[32,40,1024]{2,1,0:T(8,128)(2,1)} %all_to_all.10), kind=kOutput, calls=%fused_computation.9 | convolution fusion | flops 1342177280 | bytes 6291456 | tf_op jit(solution)/shard_map/scw,wgu->scgu/dot_general | solution.py:178
  209.6 3.4 %fusion.18 = f32[32,40,2,256]{3,1,2,0:T(8,128)S(1)} fusion(f32[32,40,2,256]{3,1,2,0:T(8,128)S(1)} %fusion.4, bf16[1024,2,256,1]{2,0,1,3:T(8,128)(2,1)S(1)} %bitcast.127, bf16[32,40,1024]{2,1,0:T(8,128)(2,1)} %collective-permute-done.2), kind=kOutput, calls=%fused_computation.30 | convolution fusion | flops 1342832640 | bytes 8912896 | tf_op jit(solution)/shard_map/scw,wgu->scgu/dot_general | solution.py:180
  213.0 1.6 convolution_convert_fusion
  214.6 2.1 constant_dynamic-slice_fusion
  216.7 1.1 copy-done.1
  218.3 4.9 %collective-permute-done.3 = bf16[32,40,1024]{2,1,0:T(8,128)(2,1)} collective-permute-done((bf16[32,40,1024]{2,1,0:T(8,128)(2,1)}, bf16[32,40,1024]{2,1,0:T(8,128)(2,1)}, u32[]{:S(2)}, u32[]{:S(2)}) %collective-permute-start.3) | collective-permute-done | bytes 2621472 | tf_op jit(solution)/shard_map/ppermute | solution.py:197
  223.2 3.7 %convert_add_fusion = f32[32,40,1024]{2,1,0:T(8,128)S(1)} fusion(bf16[32,40,1024]{2,1,0:T(8,128)(2,1)} %collective-permute-done.3, bf16[32,40,2048]{2,1,0:T(8,128)(2,1)} %copy-done.1, s32[]{:T(128)S(6)} %select_n.75), kind=kLoop, calls=%fused_computation.3 | loop fusion | flops 3932160 | bytes 10485764 | tf_op jit(solution)/shard_map/add | solution.py:197
  226.9 2.3 copy-done
  230.3 30.3 %collective-permute-done.4 = bf16[32,40,512]{2,1,0:T(8,128)(2,1)} collective-permute-done((bf16[32,40,512]{2,1,0:T(8,128)(2,1)S(1)}, bf16[32,40,512]{2,1,0:T(8,128)(2,1)}, u32[]{:S(2)}, u32[]{:S(2)}) %collective-permute-start.4) | collective-permute-done | bytes 1310752 | tf_op jit(solution)/shard_map/ppermute | solution.py:201
  260.7 2.6 add_convert_fusion
  263.3 1.2 pad_maximum_fusion
  264.5 7.8 %all-to-all-start.1 = ((bf16[64,40,256]{2,1,0:T(8,128)(2,1)}), bf16[64,40,256]{2,1,0:T(8,128)(2,1)S(1)}, u32[]{:S(2)}, u32[]{:S(2)}) async-start(bf16[64,40,256]{2,1,0:T(8,128)(2,1)} %bitcast.31), calls=%async_computation.1 | async-start | bytes 2621440 | tf_op jit(solution)/shard_map/all_to_all | solution.py:207
  275.5 32.3 %all-to-all-done.1 = bf16[64,40,256]{2,1,0:T(8,128)(2,1)S(1)} async-done(((bf16[64,40,256]{2,1,0:T(8,128)(2,1)}), bf16[64,40,256]{2,1,0:T(8,128)(2,1)S(1)}, u32[]{:S(2)}, u32[]{:S(2)}) %all-to-all-start.1) | async-done | bytes 1310752 | tf_op jit(solution)/shard_map/all_to_all | solution.py:207
  307.8 3.0 fusion.52
  (125 shorter events, 25.9 us)
Async XLA Ops:
  7.2 114.6 %all-reduce.3.cloned.1.call-start = ((), (), s32[]{:S(2)}) async-start(), calls=%async_computation.2 | async-start | bytes 2097152 | tf_op jit(solution)/shard_map/psum | solution.py:133
  8.8 4.9 %copy-start.2 = (bf16[256,2048]{1,0:T(8,128)(2,1)S(1)}, bf16[256,2048]{1,0:T(8,128)(2,1)}, u32[]{:S(2)}) copy-start(bf16[256,2048]{1,0:T(8,128)(2,1)} %param.15) | copy-start | bytes 3145732
  8.8 4.8 %copy-start.19 = (f32[2048]{0:T(1024)S(1)}, f32[2048]{0:T(1024)}, u32[]{:S(2)}) copy-start(f32[2048]{0:T(1024)} %param.21) | copy-start | bytes 24580
  13.6 4.0 %copy-start.15 = (s32[4,8]{1,0:T(4,128)S(1)}, s32[4,8]{1,0:T(4,128)}, u32[]{:S(2)}) copy-start(s32[4,8]{1,0:T(4,128)} %param.17) | copy-start | bytes 388
  13.6 4.1 %copy-start.16 = (s32[4,8]{1,0:T(4,128)S(1)}, s32[4,8]{1,0:T(4,128)}, u32[]{:S(2)}) copy-start(s32[4,8]{1,0:T(4,128)} %param.20) | copy-start | bytes 388
  13.7 4.3 %copy-start.17 = (f32[2,256]{1,0:T(2,128)S(1)}, f32[2,256]{1,0:T(2,128)}, u32[]{:S(2)}) copy-start(f32[2,256]{1,0:T(2,128)} %param.23) | copy-start | bytes 6148
  13.7 4.3 %copy-start.14 = (s32[4]{0:T(128)S(1)}, s32[4]{0:T(128)}, u32[]{:S(2)}) copy-start(s32[4]{0:T(128)} %param.18) | copy-start | bytes 52
  13.7 4.4 %copy-start.18 = (s32[4,64]{1,0:T(4,128)S(1)}, s32[4,64]{1,0:T(4,128)}, u32[]{:S(2)}) copy-start(s32[4,64]{1,0:T(4,128)} %param.19) | copy-start | bytes 3076
  16.7 0.9 copy-start.5
  16.7 4.2 %copy-start.3 = (bf16[256,2048]{1,0:T(8,128)(2,1)S(1)}, bf16[256,2048]{1,0:T(8,128)(2,1)}, u32[]{:S(2)}) copy-start(bf16[256,2048]{1,0:T(8,128)(2,1)} %param.24) | copy-start | bytes 3145732
  59.1 1.0 copy-start.6
  59.1 1.0 copy-start.7
  59.1 1.0 copy-start.9
  60.2 0.9 copy-start.8
  65.0 3.0 collective-permute-start
  70.4 2.2 copy-start.13
  70.4 2.2 copy-start.11
  70.4 2.2 copy-start.12
  123.3 1.2 collective-permute-start.1
  126.4 72.6 %copy-start.4 = (bf16[1,256,2048]{2,1,0:T(8,128)(2,1)S(1)}, bf16[1,256,2048]{2,1,0:T(8,128)(2,1)}, u32[]{:S(2)}) copy-start(bf16[1,256,2048]{2,1,0:T(8,128)(2,1)} %param.29) | copy-start | bytes 3145732
  199.0 10.6 %collective-permute-start.2 = (bf16[32,40,1024]{2,1,0:T(8,128)(2,1)}, bf16[32,40,1024]{2,1,0:T(8,128)(2,1)}, u32[]{:S(2)}, u32[]{:S(2)}) collective-permute-start(bf16[32,40,1024]{2,1,0:T(8,128)(2,1)} %all_to_all.10), channel_id=1, source_target_pairs={{0,1},{1,0},{2,3},{3,2},{4,5},{5,4},{6,7},{7,6},{8,9},{9,8},{10,11... | collective-permute-start | bytes 7864328 | tf_op jit(solution)/shard_map/ppermute | solution.py:170
  214.6 3.2 %copy-start.1 = (bf16[32,40,2048]{2,1,0:T(8,128)(2,1)}, bf16[32,40,2048]{2,1,0:T(8,128)(2,1)S(1)}, u32[]{:S(2)}) copy-start(bf16[32,40,2048]{2,1,0:T(8,128)(2,1)S(1)} %convolution_convert_fusion) | copy-start | bytes 15728644
  217.8 5.4 %collective-permute-start.3 = (bf16[32,40,1024]{2,1,0:T(8,128)(2,1)}, bf16[32,40,1024]{2,1,0:T(8,128)(2,1)}, u32[]{:S(2)}, u32[]{:S(2)}) collective-permute-start(bf16[32,40,1024]{2,1,0:T(8,128)(2,1)} %constant_dynamic-slice_fusion), channel_id=1, source_target_pairs={{0,1},{1,0},{2,3},{3,2},{4,5},{5,4},{6,7},{7,6},{8,9},{9,8},{10,11... | collective-permute-start | bytes 7864328 | tf_op jit(solution)/shard_map/ppermute | solution.py:197
  226.9 2.3 copy-start
  229.4 31.2 %collective-permute-start.4 = (bf16[32,40,512]{2,1,0:T(8,128)(2,1)S(1)}, bf16[32,40,512]{2,1,0:T(8,128)(2,1)}, u32[]{:S(2)}, u32[]{:S(2)}) collective-permute-start(bf16[32,40,512]{2,1,0:T(8,128)(2,1)S(1)} %dynamic-slice_convert_fusion), channel_id=1, source_target_pairs={{0,2},{2,0},{1,3},{3,1},{4,6},{6,4},{5,7},{7,5},{8,10},{10,8},{9,1... | collective-permute-start | bytes 3932168 | tf_op jit(solution)/shard_map/ppermute | solution.py:201
  264.5 43.3 %copy-start.10 = (f32[256,64]{0,1:T(8,128)S(1)}, f32[256,64]{0,1:T(8,128)}, u32[]{:S(2)}) copy-start(f32[256,64]{0,1:T(8,128)} %get-tuple-element.4) | copy-start | bytes 196612
  264.5 43.3 %all-to-all-start.1 = ((bf16[64,40,256]{2,1,0:T(8,128)(2,1)}), bf16[64,40,256]{2,1,0:T(8,128)(2,1)S(1)}, u32[]{:S(2)}, u32[]{:S(2)}) async-start(bf16[64,40,256]{2,1,0:T(8,128)(2,1)} %bitcast.31), calls=%async_computation.1 | async-start | bytes 2621440 | tf_op jit(solution)/shard_map/all_to_all | solution.py:207
Sparse Core Ops, SparseCore 0:
  70.5 51.2 all-reduce.2
